TPU v7x, 256 devices: a whole 4x4x8 slice. The times are simulated.
256 devices in a mesh: seq: 64 (over x, z, core), tensor: 4 (over y).
Axes of the slice: x: 4, y: 4, z: 8, core: 2. Of those that a mesh axis runs over, the one named last changes fastest.
Arguments:
- hidden: bfloat16 [512, 1280], P('seq', 'tensor'), may hold values from -20 to 20
- inward_weight: bfloat16 [1280, 3, 1280], P(None, None, 'tensor'), may hold values from -0.15625 to 0.15625
- output_weight: bfloat16 [1280, 1280], P('tensor'), may hold values from -0.559017 to 0.559017
- score_gain: float32 [1280], P('tensor'), may hold values from 0.5 to 9
- eigen_rate: float32 [1280], replicated, may hold values from 0.1 to 0.6
- lengths: int32 [512], replicated, may hold values from 1 to 16384, as said below
- page_request: int32 [1536], P('seq'), may hold values from 0 to 511, as said below
- page_number: int32 [1536], P('seq'), may hold values from 0 to 128, as said below
- page_cache: bfloat16 [1536, 128, 2, 1280], P('seq', None, None, 'tensor'), may hold values from -6 to 6
Outputs:
- new_hidden: bfloat16 [512, 1280], P('seq', 'tensor')
Inputs may be any that keep to these rules, and one draw needn't show every extreme that they name: `lengths`: exactly 4 requests have more than 256 cached positions; they have more than 16256, one has exactly 16384. Every other request has at most 256, one exactly 256. `page_request`: each page of each request stands in exactly one slot: pages 0 to 1 of every short request, pages 0 to 127 of every long request. The remaining 2 * 4 slots name a long request with page number 128 and hold nothing live. `page_number`: see page_request.
All inputs are finite; a program needn't handle non-finite values.
Results may differ from a plain program's by a relative error of at most 0.012.
The roundings to bfloat16 on the way count: a program that leaves them out, or rounds other values in their place, can miss the bound.
Values may be sent and summed in bfloat16 or wider, within the bound.
No kernel may reach another device: no remote copies, remote signals or barrier semaphores. Data moves between devices by JAX's collectives and lax.ppermute only.
A program may use at most 192 MiB of HBM per device.

v0:
```python
import math
import jax
import jax.numpy as jnp
from jax import lax
from jax.sharding import PartitionSpec as P

HEAD_DIM = 64
epsilon = 1e-06
far_below = -1e30


def merged_2(part, axis, combine):
    gathered = jax.tree.map(lambda a: lax.all_gather(a, axis), part)

    def take(source):
        return jax.tree.map(lambda a: lax.dynamic_index_in_dim(a, source, 0, False), gathered)

    return lax.fori_loop(
        1, lax.axis_size(axis), lambda source, state: combine(state, take(source)), take(0)
    )


def head_norm(values, gain):
    shaped = values.reshape(values.shape[:-1] + (-1, HEAD_DIM))
    normed = shaped / jnp.sqrt(jnp.mean(shaped * shaped, axis=-1, keepdims=True) + epsilon)
    return normed * gain.reshape(-1, HEAD_DIM)


def scale_heads(summed, factor):
    shaped = summed.reshape(summed.shape[:-1] + (factor.shape[-1], -1))
    return (shaped * factor[..., None]).reshape(summed.shape)


def join_parts(first, second):
    first_max, first_total, first_acc = first
    second_max, second_total, second_acc = second
    top = jnp.maximum(first_max, second_max)
    first_factor = jnp.exp(first_max - top)
    second_factor = jnp.exp(second_max - top)
    return (
        top,
        first_total * first_factor + second_total * second_factor,
        scale_heads(first_acc, first_factor) + scale_heads(second_acc, second_factor),
    )


def local(
    hidden,
    inward_weight,
    output_weight,
    score_gain,
    eigen_rate,
    lengths,
    page_request,
    page_number,
    page_cache,
):
    rows, width_local = hidden.shape
    heads_local = width_local // HEAD_DIM
    gathered = lax.all_gather(hidden, "tensor", axis=1, tiled=True)
    projected = jnp.dot(
        gathered,
        inward_weight.reshape(inward_weight.shape[0], -1),
        preferred_element_type=jnp.float32,
    )
    query = head_norm(projected[:, :width_local], score_gain).astype(jnp.bfloat16)
    key_new = head_norm(projected[:, width_local : 2 * width_local], score_gain).astype(
        jnp.bfloat16
    )
    value_own = projected[:, 2 * width_local :].astype(jnp.bfloat16)
    own_score = jnp.sum(
        query.astype(jnp.float32) * key_new.astype(jnp.float32), axis=-1
    ) / math.sqrt(HEAD_DIM)
    all_queries = lax.all_gather(query.reshape(rows, width_local), "seq", axis=0, tiled=True)
    pages, page_len = (page_cache.shape[0], page_cache.shape[1])
    owner_query = all_queries[page_request].reshape(pages, heads_local, HEAD_DIM)
    keys_scaled = head_norm(page_cache[:, :, 0, :].astype(jnp.float32), score_gain).astype(
        jnp.bfloat16
    )
    values_paged = page_cache[:, :, 1, :].reshape(pages, page_len, heads_local, HEAD_DIM)
    scores = jnp.einsum(
        "sphd,shd->shp", keys_scaled, owner_query, preferred_element_type=jnp.float32
    ) / math.sqrt(HEAD_DIM)
    positions = page_number[:, None] * page_len + jnp.arange(page_len, dtype=jnp.int32)[None, :]
    live_mask = positions < lengths[page_request][:, None]
    page_max = jnp.max(jnp.where(live_mask[:, None, :], scores, far_below), axis=-1)
    weights = jnp.where(live_mask[:, None, :], jnp.exp(scores - page_max[..., None]), 0.0).astype(
        jnp.bfloat16
    )
    page_total = jnp.sum(weights.astype(jnp.float32), axis=-1)
    page_acc = jnp.einsum(
        "shp,sphd->shd", weights, values_paged, preferred_element_type=jnp.float32
    ).reshape(pages, width_local)
    requests = lengths.shape[0]
    onehot = page_request[:, None] == jnp.arange(requests, dtype=jnp.int32)[None, :]
    request_max = jnp.max(jnp.where(onehot[:, :, None], page_max[:, None, :], far_below), axis=0)
    factor = jnp.exp(page_max - request_max[page_request])
    selector = onehot.astype(jnp.float32)
    request_total = jnp.dot(selector.T, page_total * factor, precision=lax.Precision.HIGHEST)
    request_acc = jnp.dot(
        selector.T, scale_heads(page_acc, factor), precision=lax.Precision.HIGHEST
    )
    first_row = lax.axis_index("seq") * rows
    merged = merged_2((request_max, request_total, request_acc), "seq", join_parts)
    home_max = lax.dynamic_slice_in_dim(merged[0], first_row, rows, 0)
    home_total = lax.dynamic_slice_in_dim(merged[1], first_row, rows, 0)
    home_acc = lax.dynamic_slice_in_dim(merged[2], first_row, rows, 0)
    final_max = jnp.maximum(home_max, own_score)
    stored_factor = jnp.exp(home_max - final_max)
    own_factor = jnp.exp(own_score - final_max)
    total = home_total * stored_factor + own_factor
    summed = scale_heads(home_acc, stored_factor) + scale_heads(
        value_own.astype(jnp.float32), own_factor
    )
    attended = (
        (summed.reshape(rows, heads_local, HEAD_DIM) / total[..., None])
        .reshape(rows, width_local)
        .astype(jnp.bfloat16)
    )
    partial_out = jnp.dot(attended, output_weight, preferred_element_type=jnp.float32)
    first_col = lax.axis_index("tensor") * width_local
    rate = lax.dynamic_slice_in_dim(eigen_rate, first_col, width_local, 0)
    state = hidden.astype(jnp.float32)
    width = partial_out.shape[1]
    attn_local = lax.psum_scatter(partial_out, "tensor", scatter_dimension=1, tiled=True)
    attn_square = lax.psum(jnp.sum(attn_local * attn_local, axis=-1), "tensor")
    unit = attn_local / jnp.sqrt(attn_square / width + epsilon)[:, None]
    mixed = state + rate * (unit - state)
    mixed_square = lax.psum(jnp.sum(mixed * mixed, axis=-1), "tensor")
    return (mixed / jnp.sqrt(mixed_square / width + epsilon)[:, None]).astype(jnp.bfloat16)


def solution(mesh):
    placed = (
        P("seq", "tensor"),
        P(None, None, "tensor"),
        P("tensor", None),
        P("tensor"),
        P(),
        P(),
        P("seq"),
        P("seq"),
        P("seq", None, None, "tensor"),
    )
    return jax.shard_map(
        local, mesh=mesh, in_specs=placed, out_specs=P("seq", "tensor"), check_vma=False
    )
```

profile of v0, /device:TPU:2, one launch (start us, length us, event | category | flops | bytes accessed | tf_op | source)
XLA Modules:
  0.0 608.3 jit_solution(11876755678239287850)
XLA Ops:
  8.1 12.7 %all-gather.3 = bf16[4,320,8]{1,2,0:T(8,128)(2,1)S(1)} all-gather(bf16[1,320,8]{1,2,0:T(8,128)(2,1)} %bitcast.78), channel_id=1, replica_groups=mesh['seq'=64,'tensor'=4] {'tensor'}, dimensions={0}, use_global_device_ids=true | all-gather | bytes 25600 | tf_op jit(solution)/shard_map/all_gather | solution.py:60
  22.1 50.5 %all_gather.25 = bf16[512,320]{1,0:T(8,128)(2,1)S(1)} all-gather(bf16[8,320]{1,0:T(8,128)(2,1)S(1)} %get-tuple-element.242), channel_id=1, replica_groups=mesh['seq'=64,'tensor'=4] {'seq'}, dimensions={0}, use_global_device_ids=true | all-gather | bytes 332800 | tf_op jit(solution)/shard_map/all_gather | solution.py:74
  73.3 3.7 fusion.24
  85.1 50.0 %all-gather.1 = f32[32768,5]{0,1:T(8,128)S(1)} all-gather(f32[512,5]{0,1:T(8,128)S(1)} %fusion.12), channel_id=3, replica_groups=mesh['seq'=64,'tensor'=4] {'seq'}, dimensions={0}, use_global_device_ids=true | all-gather | bytes 665600 | tf_op jit(solution)/shard_map/all_gather | solution.py:13
  135.1 50.6 %all-gather = f32[32768,5]{0,1:T(8,128)S(1)} all-gather(f32[512,5]{0,1:T(8,128)S(1)} %select_reduce_fusion), channel_id=2, replica_groups=mesh['seq'=64,'tensor'=4] {'seq'}, dimensions={0}, use_global_device_ids=true | all-gather | bytes 665600 | tf_op jit(solution)/shard_map/all_gather | solution.py:13
  187.0 62.2 %all-gather.6.cloned.1.call-done = f32[32768,320]{0,1:T(8,128)} async-done(((f32[512,320]{0,1:T(8,128)}), f32[32768,320]{0,1:T(8,128)}) %all-gather.6.cloned.1.call-update) | async-done | bytes 41943056 | tf_op jit(solution)/shard_map/all_gather | solution.py:13
  249.1 38.8 %copy.54 = f32[40,8,64,512]{3,2,1,0:T(8,128)} copy(f32[40,8,64,512]{3,1,2,0:T(8,128)} %bitcast.71) | data formatting | bytes 83886080
  289.0 265.0 %while.19 = (s32[]{:T(128)}, f32[512,5]{0,1:T(8,128)S(1)}, f32[512,5]{0,1:T(8,128)S(1)}, f32[512,320]{0,1:T(8,128)S(1)}, f32[64,512,5]{1,2,0:T(8,128)}, /*index=...) while((s32[]{:T(128)}, f32[512,5]{0,1:T(8,128)S(1)}, ...), condition=%wide.region_6.7_spmd, body=%wide.region_5.6_spmd.sunk | while | flops 506885 | bytes 3379351 | solution.py:18
  289.8 3.1 constant_dynamic-slice_fusion.2
  298.2 3.1 constant_dynamic-slice_fusion.2
  306.6 3.1 constant_dynamic-slice_fusion.2
  315.0 3.1 constant_dynamic-slice_fusion.2
  323.4 3.1 constant_dynamic-slice_fusion.2
  327.6 3.1 constant_dynamic-slice_fusion.2
  336.1 3.1 constant_dynamic-slice_fusion.2
  344.5 3.1 constant_dynamic-slice_fusion.2
  352.9 3.1 constant_dynamic-slice_fusion.2
  361.3 3.1 constant_dynamic-slice_fusion.2
  369.7 3.1 constant_dynamic-slice_fusion.2
  378.1 3.1 constant_dynamic-slice_fusion.2
  386.5 3.1 constant_dynamic-slice_fusion.2
  558.5 22.7 %reduce-scatter.4.cloned.1.call-done = f32[320,8]{1,0:T(8,128)} async-done(((f32[1280,8]{1,0:T(8,128)}), f32[320,8]{1,0:T(8,128)}) %reduce-scatter.4.cloned.1.call-update) | async-done | bytes 10256
  583.1 8.3 %psum.14 = f32[8]{0:T(128)S(1)} all-reduce(f32[8]{0:T(128)S(1)} %multiply_reduce_fusion.4), channel_id=1, replica_groups=mesh['seq'=64,'tensor'=4] {'tensor'}, use_global_device_ids=true, to_apply=%region_11.12 | all-reduce | flops 8 | bytes 64 | tf_op jit(solution)/shard_map/psum | solution.py:126
  591.6 9.2 %psum.15 = f32[8]{0:T(128)S(1)} all-reduce(f32[8]{0:T(128)S(1)} %get-tuple-element.232), channel_id=1, replica_groups=mesh['seq'=64,'tensor'=4] {'tensor'}, use_global_device_ids=true, to_apply=%region_13.14 | all-reduce | flops 8 | bytes 64 | tf_op jit(solution)/shard_map/psum | solution.py:129
  (256 shorter events, 243.7 us)
Async XLA Ops:
  6.5 14.3 %copy-start = (bf16[1280,3,320]{0,2,1:T(8,128)(2,1)S(1)}, bf16[1280,3,320]{0,2,1:T(8,128)(2,1)}, u32[]{:S(2)}) copy-start(bf16[1280,3,320]{0,2,1:T(8,128)(2,1)} %param.12) | copy-start | bytes 7372804
  6.5 15.5 %copy-start.5 = (f32[320]{0:T(512)S(1)}, f32[320]{0:T(512)}, u32[]{:S(2)}) copy-start(f32[320]{0:T(512)} %param.14) | copy-start | bytes 3844
  6.5 242.6 %all-gather.6.cloned.1.call-start = ((), (), s32[]{:S(2)}) async-start(), calls=%async_computation.1 | async-start | bytes 42598400 | tf_op jit(solution)/shard_map/all_gather | solution.py:13
  77.0 0.7 copy-start.2
  77.0 1.5 copy-start.7
  79.3 4.1 copy-start.6
  84.7 496.5 %reduce-scatter.4.cloned.1.call-start = ((), (), s32[]{:S(2)}) async-start(), calls=%async_computation.2 | async-start | bytes 819200
  185.6 1.0 copy-start.3
  554.0 37.4 %copy-start.4 = (bf16[8,320]{1,0:T(8,128)(2,1)S(1)}, bf16[8,320]{1,0:T(8,128)(2,1)}, u32[]{:S(2)}) copy-start(bf16[8,320]{1,0:T(8,128)(2,1)} %param.11) | copy-start | bytes 15364
  554.0 47.5 %copy-start.1 = (bf16[1280,3,320]{0,2,1:T(8,128)(2,1)S(1)}, bf16[1280,3,320]{0,2,1:T(8,128)(2,1)}, u32[]{:S(2)}) copy-start(bf16[1280,3,320]{0,2,1:T(8,128)(2,1)} %param.12) | copy-start | bytes 7372804
Sparse Core Ops, SparseCore 0:
  84.8 164.2 all-gather.5
  558.6 22.5 reduce-scatter.3
where the time goes:
time: 615 us; the launch traced here: 608 us
  local copies, waits for them, and re-layouts  249 us (40%)
  blocking collectives  181 us (29%)
  waiting for transfers between devices  84.9 us (14%)
  other arithmetic  69.5 us (11%)
  between operations  13.6 us (2%)
  matrix products  8.17 us (1%)
    dynamic_slice x66, local copies, waits for them, and re-layouts, take(): lax.dynamic_index_in_dim(a, source, 0, False)  199 us
    all_gather x2, blocking collectives, merged_2(): gathered = jax.tree.map(lambda a: lax.all_gather(a, axis), part)  101 us
    all_gather x1, waiting for transfers between devices, merged_2(): gathered = jax.tree.map(lambda a: lax.all_gather(a, axis), part)  62.2 us
    all_gather x1, blocking collectives, local(): lax.all_gather(query.reshape(rows, width_local), 'seq', axis=0, tiled=True)  50.5 us
    add x63, other arithmetic, join_parts(): first_total * first_factor + second_total * second_factor  46.9 us
    unnamed x19, local copies, waits for them, and re-layouts  40.9 us
    unnamed x3, waiting for transfers between devices  22.8 us
    add x63, other arithmetic, join_parts(): scale_heads(first_acc, first_factor)  18.3 us
  transfers between devices with their start and end apart: 2, of which 2 were waited for; matrix products, arithmetic and copies ran while one was open for 0% of the time, Pallas kernels for 0%

commit v1 on v0

--- a/solution.py
+++ b/solution.py
@@ -7,6 +7,13 @@
 HEAD_DIM = 64
 epsilon = 1e-06
 far_below = -1e30
+
+
+def gather_over(value, axis, dim):
+    n_dev = lax.axis_size(axis)
+    blocks = jnp.stack([value for _ in range(n_dev)])
+    blocks = lax.all_to_all(blocks, axis, split_axis=0, concat_axis=0)
+    return jnp.concatenate(blocks, axis=dim)
 
 
 def merged_2(part, axis, combine):
@@ -71,7 +78,7 @@
     own_score = jnp.sum(
         query.astype(jnp.float32) * key_new.astype(jnp.float32), axis=-1
     ) / math.sqrt(HEAD_DIM)
-    all_queries = lax.all_gather(query.reshape(rows, width_local), "seq", axis=0, tiled=True)
+    all_queries = gather_over(query.reshape(rows, width_local), "seq", 0)
     pages, page_len = (page_cache.shape[0], page_cache.shape[1])
     owner_query = all_queries[page_request].reshape(pages, heads_local, HEAD_DIM)
     keys_scaled = head_norm(page_cache[:, :, 0, :].astype(jnp.float32), score_gain).astype(

time: 615 us -> 583 us (0.948)
  blocking collectives: 181 us -> 136 us
  starting transfers between devices: 0.04 us -> 12.1 us
    all_gather x1 -> x0, blocking collectives: 50.5 us -> none  [local(): lax.all_gather(query.reshape(rows, width_local), 'seq', axis=0, tiled=True)]
    all_to_all x0 -> x1, starting transfers between devices: none -> 12 us  [gather_over(): blocks = lax.all_to_all(blocks, axis, split_axis=0, concat_axis=0)]
    all_to_all x0 -> x1, waiting for transfers between devices: none -> 8.62 us  [gather_over(): blocks = lax.all_to_all(blocks, axis, split_axis=0, concat_axis=0)]
    all_gather x1, waiting for transfers between devices: 62.2 us -> 55.8 us  [merged_2(): gathered = jax.tree.map(lambda a: lax.all_gather(a, axis), part)]
    unnamed x19 -> x17, local copies, waits for them, and re-layouts: 40.9 us -> 39.9 us
  transfers between devices with their start and end apart: 2 -> 3, of which waited for: 2 -> 3; matrix products, arithmetic and copies ran while one was open for 0% -> 1% of each run, Pallas kernels for 0% -> 0%
where the time goes in v1:
time: 583 us; the launch traced here: 576 us
  local copies, waits for them, and re-layouts  250 us (43%)
  blocking collectives  136 us (23%)
  waiting for transfers between devices  87.3 us (15%)
  other arithmetic  68 us (12%)
  between operations  13.6 us (2%)
  starting transfers between devices  12.1 us (2%)
  matrix products  8.15 us (1%)
    dynamic_slice x66, local copies, waits for them, and re-layouts, take(): lax.dynamic_index_in_dim(a, source, 0, False)  200 us
    all_gather x2, blocking collectives, merged_2(): gathered = jax.tree.map(lambda a: lax.all_gather(a, axis), part)  105 us
    all_gather x1, waiting for transfers between devices, merged_2(): gathered = jax.tree.map(lambda a: lax.all_gather(a, axis), part)  55.8 us
    add x63, other arithmetic, join_parts(): first_total * first_factor + second_total * second_factor  46.7 us
    unnamed x17, local copies, waits for them, and re-layouts  39.9 us
    unnamed x3, waiting for transfers between devices  22.9 us
    add x63, other arithmetic, join_parts(): scale_heads(first_acc, first_factor)  18.3 us
    all_gather x1, blocking collectives, local(): gathered = lax.all_gather(hidden, 'tensor', axis=1, tiled=True)  12.8 us
  transfers between devices with their start and end apart: 3, of which 3 were waited for; matrix products, arithmetic and copies ran while one was open for 1% of the time, Pallas kernels for 0%

profile of v1, /device:TPU:2, one launch (start us, length us, event | category | flops | bytes accessed | tf_op | source)
XLA Modules:
  0.0 576.2 jit_solution(13078112070488191125)
XLA Ops:
  6.5 12.8 %all-gather.3 = bf16[4,320,8]{1,2,0:T(8,128)(2,1)S(1)} all-gather(bf16[1,320,8]{1,2,0:T(8,128)(2,1)} %bitcast.79), channel_id=1, replica_groups=mesh['seq'=64,'tensor'=4] {'tensor'}, dimensions={0}, use_global_device_ids=true | all-gather | bytes 25600 | tf_op jit(solution)/shard_map/all_gather | solution.py:67
  21.5 12.0 %all-to-all-start = ((bf16[64,8,320]{2,1,0:T(8,128)(2,1)}), bf16[64,8,320]{2,1,0:T(8,128)(2,1)S(1)}, u32[]{:S(2)}, u32[]{:S(2)}) async-start(bf16[64,8,320]{2,1,0:T(8,128)(2,1)} %stack.3), calls=%async_computation | async-start | bytes 786432 | tf_op jit(solution)/shard_map/all_to_all | solution.py:15
  33.7 3.7 fusion.24
  39.0 8.6 %all-to-all-done = bf16[64,8,320]{2,1,0:T(8,128)(2,1)S(1)} async-done(((bf16[64,8,320]{2,1,0:T(8,128)(2,1)}), bf16[64,8,320]{2,1,0:T(8,128)(2,1)S(1)}, u32[]{:S(2)}, u32[]{:S(2)}) %all-to-all-start) | async-done | bytes 327712 | tf_op jit(solution)/shard_map/all_to_all | solution.py:15
  55.1 49.3 %all-gather.1 = f32[32768,5]{0,1:T(8,128)S(1)} all-gather(f32[512,5]{0,1:T(8,128)S(1)} %fusion.12), channel_id=3, replica_groups=mesh['seq'=64,'tensor'=4] {'seq'}, dimensions={0}, use_global_device_ids=true | all-gather | bytes 665600 | tf_op jit(solution)/shard_map/all_gather | solution.py:20
  104.4 56.1 %all-gather = f32[32768,5]{0,1:T(8,128)} all-gather(f32[512,5]{0,1:T(8,128)S(1)} %select_reduce_fusion), channel_id=2, replica_groups=mesh['seq'=64,'tensor'=4] {'seq'}, dimensions={0}, use_global_device_ids=true | all-gather | bytes 665600 | tf_op jit(solution)/shard_map/all_gather | solution.py:20
  161.2 55.8 %all-gather.6.cloned.1.call-done = f32[32768,320]{0,1:T(8,128)} async-done(((f32[512,320]{0,1:T(8,128)}), f32[32768,320]{0,1:T(8,128)}) %all-gather.6.cloned.1.call-update) | async-done | bytes 41943056 | tf_op jit(solution)/shard_map/all_gather | solution.py:20
  216.9 38.8 %copy.54 = f32[40,8,64,512]{3,2,1,0:T(8,128)} copy(f32[40,8,64,512]{3,1,2,0:T(8,128)} %bitcast.72) | data formatting | bytes 83886080
  256.8 264.8 %while.19 = (s32[]{:T(128)}, f32[512,5]{0,1:T(8,128)S(1)}, f32[512,5]{0,1:T(8,128)S(1)}, f32[512,320]{0,1:T(8,128)S(1)}, f32[64,512,5]{1,2,0:T(8,128)}, /*index=...) while((s32[]{:T(128)}, f32[512,5]{0,1:T(8,128)S(1)}, ...), condition=%wide.region_6.7_spmd, body=%wide.region_5.6_spmd.sunk | while | flops 506885 | bytes 3379351 | solution.py:25
  257.6 3.1 constant_dynamic-slice_fusion.2
  270.2 3.1 constant_dynamic-slice_fusion.2
  274.4 3.1 constant_dynamic-slice_fusion.2
  278.6 3.1 constant_dynamic-slice_fusion.2
  291.2 3.1 constant_dynamic-slice_fusion.2
  295.4 3.1 constant_dynamic-slice_fusion.2
  312.2 3.1 constant_dynamic-slice_fusion.2
  316.5 3.1 constant_dynamic-slice_fusion.2
  329.1 3.1 constant_dynamic-slice_fusion.2
  333.3 3.1 constant_dynamic-slice_fusion.2
  337.5 3.1 constant_dynamic-slice_fusion.2
  350.1 3.1 constant_dynamic-slice_fusion.2
  526.2 22.9 %reduce-scatter.4.cloned.1.call-done = f32[320,8]{1,0:T(8,128)} async-done(((f32[1280,8]{1,0:T(8,128)}), f32[320,8]{1,0:T(8,128)}) %reduce-scatter.4.cloned.1.call-update) | async-done | bytes 10256
  551.0 8.3 %psum.14 = f32[8]{0:T(128)S(1)} all-reduce(f32[8]{0:T(128)S(1)} %multiply_reduce_fusion.4), channel_id=1, replica_groups=mesh['seq'=64,'tensor'=4] {'tensor'}, use_global_device_ids=true, to_apply=%region_11.12 | all-reduce | flops 8 | bytes 64 | tf_op jit(solution)/shard_map/psum | solution.py:133
  559.5 9.1 %psum.15 = f32[8]{0:T(128)S(1)} all-reduce(f32[8]{0:T(128)S(1)} %get-tuple-element.232), channel_id=1, replica_groups=mesh['seq'=64,'tensor'=4] {'tensor'}, use_global_device_ids=true, to_apply=%region_13.14 | all-reduce | flops 8 | bytes 64 | tf_op jit(solution)/shard_map/psum | solution.py:136
  (256 shorter events, 245.8 us)
Async XLA Ops:
  6.5 12.9 %copy-start = (bf16[1280,3,320]{0,2,1:T(8,128)(2,1)S(1)}, bf16[1280,3,320]{0,2,1:T(8,128)(2,1)}, u32[]{:S(2)}) copy-start(bf16[1280,3,320]{0,2,1:T(8,128)(2,1)} %param.12) | copy-start | bytes 7372804
  6.5 14.0 %copy-start.4 = (f32[320]{0:T(512)S(1)}, f32[320]{0:T(512)}, u32[]{:S(2)}) copy-start(f32[320]{0:T(512)} %param.14) | copy-start | bytes 3844
  6.5 27.1 %copy-start.5 = (s32[24]{0:T(128)S(1)}, s32[24]{0:T(128)}, u32[]{:S(2)}) copy-start(s32[24]{0:T(128)} %param.17) | copy-start | bytes 292
  21.5 26.1 %all-to-all-start = ((bf16[64,8,320]{2,1,0:T(8,128)(2,1)}), bf16[64,8,320]{2,1,0:T(8,128)(2,1)S(1)}, u32[]{:S(2)}, u32[]{:S(2)}) async-start(bf16[64,8,320]{2,1,0:T(8,128)(2,1)} %stack.3), calls=%async_computation | async-start | bytes 786432 | tf_op jit(solution)/shard_map/all_to_all | solution.py:15
  33.5 183.4 %all-gather.6.cloned.1.call-start = ((), (), s32[]{:S(2)}) async-start(), calls=%async_computation.2 | async-start | bytes 42598400 | tf_op jit(solution)/shard_map/all_gather | solution.py:20
  33.7 3.7 copy-start.6
  33.7 3.7 copy-start.2
  54.4 494.6 %reduce-scatter.4.cloned.1.call-start = ((), (), s32[]{:S(2)}) async-start(), calls=%async_computation.3 | async-start | bytes 819200
  521.7 37.6 %copy-start.3 = (bf16[8,320]{1,0:T(8,128)(2,1)S(1)}, bf16[8,320]{1,0:T(8,128)(2,1)}, u32[]{:S(2)}) copy-start(bf16[8,320]{1,0:T(8,128)(2,1)} %param.11) | copy-start | bytes 15364
  521.7 47.6 %copy-start.1 = (bf16[1280,3,320]{0,2,1:T(8,128)(2,1)S(1)}, bf16[1280,3,320]{0,2,1:T(8,128)(2,1)}, u32[]{:S(2)}) copy-start(bf16[1280,3,320]{0,2,1:T(8,128)(2,1)} %param.12) | copy-start | bytes 7372804
Sparse Core Ops, SparseCore 0:
  54.5 162.3 all-gather.5
  526.3 22.7 reduce-scatter.3
